TPU v7x, 256 devices: a whole 4x4x8 slice. The times are simulated.
256 devices in a mesh: req: 16 (over z, core), head: 16 (over x, y).
Axes of the slice: x: 4, y: 4, z: 8, core: 2. Of those that a mesh axis runs over, the one named last changes fastest.
Arguments:
- tree_heads: bfloat16 [4096, 16384], P(('req', 'head')), may hold values from -6 to 6
- tree_gates: bfloat16 [4096, 16384], P(('req', 'head')), may hold values from -6 to 6
- tree_steps: bfloat16 [4096, 256], P(('req', 'head')), may hold values from -6 to 6
- tree_groups: bfloat16 [4096, 4096], P(('req', 'head')), may hold values from -6 to 6
- new_tree: int32 [128, 32, 32], P('req'), may hold values from 0 to 1, as said below
- kernel_heads: bfloat16 [4, 16384], P(None, 'head'), may hold values from -3 to 3
- shift_heads: float32 [16384], P('head'), may hold values from -3 to 3
- kernel_groups: bfloat16 [4, 4096], replicated, may hold values from -3 to 3
- shift_groups: float32 [4096], replicated, may hold values from -3 to 3
- log_rates: float32 [256], P('head'), may hold values from 0 to 2.77
- step_bias: float32 [256], P('head'), may hold values from -6 to -2
- skip_gain: float32 [256], P('head'), may hold values from 0.5 to 1.5
- norm_gain: float32 [16384], P('head'), may hold values from 0.5 to 1.5
- old_state: bfloat16 [128, 256, 64, 256], P('req', 'head'), may hold values from -0.59765625 to 0.59765625
- old_heads: bfloat16 [128, 32, 16384], P('req', None, 'head'), may hold values from -3 to 3
- old_keys: bfloat16 [128, 32, 2048], P('req'), may hold values from -3 to 3
- old_steps: float32 [128, 32, 256], P('req', None, 'head'), may hold values from 0.002 to 0.2
- prior_heads: bfloat16 [128, 32, 16384], P('req', None, 'head'), may hold values from -6 to 6
- prior_groups: bfloat16 [128, 32, 4096], P('req', 'head'), may hold values from -6 to 6
- old_tree: int32 [128, 32, 32], P('req'), may hold values from 0 to 1, as said below
- accepted: int32 [128], P('req'), may hold values from 2 to 31, as said below
- new_owner: int32 [128], replicated, may hold values from 0 to 127, as said below
Outputs:
- mixed: bfloat16 [4096, 16384], P('req', 'head')
Inputs may be any that keep to these rules, and one draw needn't show every extreme that they name: `old_tree`: entry (t, j) is 1 when node j is node t or one of its ancestors, else 0; node 0 is the root, every parent has a lower number than its child, node 1 is the child of node 0 and node 2 the child of node 1, and every node numbered 2 or more has depth two or more. `new_tree`: ancestor masks of the same kind as old_tree. The accepted node has depth two or more in old_tree. A permutation of the slots. Slot i lives on device i // 8 of req before and on device new_owner[i] // 8 after; no old device hands more than 2 requests to one new device, and in every draw some pairs of devices carry exactly 2.
All inputs are finite; a program needn't handle non-finite values.
Results may differ from a plain program's by a relative error of at most 0.0052.
Values may be sent and summed in bfloat16 or wider, within the bound.
No kernel may reach another device: no remote copies, remote signals or barrier semaphores. Data moves between devices by JAX's collectives and lax.ppermute only.
A program may use at most 128 MiB of HBM per device.

v0:
```python
import jax
import jax.numpy as jnp
from jax import lax
from jax.sharding import PartitionSpec as P

HEADS = 256
HEAD_DIM = 64
STATE = 256
GROUPS = 8
NODES = 32
MOST = 2
EPSILON = 1e-05


def tree_conv(tree_rows, tail_rows, ancestry, weight, offset_bias):
    node_depth = jnp.sum(ancestry, axis=-1) - 1
    places = jnp.arange(3, dtype=jnp.int32)
    summed = weight[3].astype(jnp.float32) * tree_rows.astype(jnp.float32) + offset_bias
    for upward in range(1, 4):
        picked = (
            (ancestry == 1) & (node_depth[:, None, :] == node_depth[:, :, None] - upward)
        ).astype(jnp.bfloat16)
        older_rows = (places[None, None, :] == node_depth[:, :, None] - upward + 3).astype(
            jnp.bfloat16
        )
        shifted = jnp.einsum("btj,bjc->btc", picked, tree_rows, preferred_element_type=jnp.float32)
        shifted = shifted + jnp.einsum(
            "bti,bic->btc", older_rows, tail_rows, preferred_element_type=jnp.float32
        )
        summed = summed + weight[3 - upward].astype(jnp.float32) * shifted
    return jax.nn.silu(summed).astype(jnp.bfloat16)


def place_slots(payload, positions, count):
    wanted = jnp.arange(count, dtype=jnp.int32)
    owners = jnp.arange(positions.shape[0], dtype=jnp.int32)
    hits = positions[None, :] == wanted[:, None]
    chosen = jnp.sum(jnp.where(hits, owners[None, :], 0), axis=1)
    filled = jnp.any(hits, axis=1).reshape((count,) + (1,) * (payload.ndim - 1))
    taken = jnp.take(payload, chosen, axis=0)
    return jnp.where(filled, taken, jnp.zeros_like(taken))


def shards(
    tree_heads,
    tree_gates,
    tree_steps,
    tree_groups,
    new_tree,
    kernel_heads,
    shift_heads,
    kernel_groups,
    shift_groups,
    log_rates,
    step_bias,
    skip_gain,
    norm_gain,
    old_state,
    old_heads,
    old_keys,
    old_steps,
    prior_heads,
    prior_groups,
    old_tree,
    accepted,
    new_owner,
):
    req_count = lax.axis_size("req")
    req_index = lax.axis_index("req")
    head_index = lax.axis_index("head")
    reqs_dev = new_tree.shape[0]
    local_heads = log_rates.shape[0]
    local_nodes = prior_groups.shape[1]
    per_group = HEADS // GROUPS
    span_heads = min(local_heads, per_group)
    span_groups = local_heads // span_heads
    first_group = head_index * local_heads // per_group
    slot_count = req_count * MOST
    key_width = GROUPS * STATE
    highest = lax.Precision.HIGHEST
    owner_table = new_owner.reshape(req_count, reqs_dev)
    target_dev = owner_table // reqs_dev
    local_ids = jnp.arange(reqs_dev, dtype=jnp.int32)
    before = local_ids[None, :, None] > local_ids[None, None, :]
    same_dest = target_dev[:, :, None] == target_dev[:, None, :]
    arrival = jnp.sum((same_dest & before).astype(jnp.int32), axis=-1)
    send_table = target_dev * MOST + arrival
    send_pos = lax.dynamic_index_in_dim(send_table, req_index, 0, keepdims=False)
    wanted_slot = req_index * reqs_dev + local_ids
    all_ids = jnp.arange(new_owner.shape[0], dtype=jnp.int32)
    match = new_owner[None, :] == wanted_slot[:, None]
    anchor = jnp.sum(jnp.where(match, all_ids[None, :], 0), axis=1)
    recv_pos = anchor // reqs_dev * MOST + jnp.take(arrival.reshape(-1), anchor)
    decay_rates = -jnp.exp(log_rates)
    node_ids = jnp.arange(NODES, dtype=jnp.int32)
    chosen_hot = node_ids[None, :] == accepted[:, None]
    chosen_row = jnp.sum(jnp.where(chosen_hot[:, :, None], old_tree, 0), axis=1)
    old_depth = jnp.sum(old_tree, axis=-1) - 1
    chosen_depth = jnp.sum(jnp.where(chosen_hot, old_depth, 0), axis=1)
    places = jnp.arange(3, dtype=jnp.int32)
    lineage = chosen_row == 1
    tail_pick = (
        lineage[:, None, :]
        & (old_depth[:, None, :] == chosen_depth[:, None, None] - 2 + places[None, :, None])
    ).astype(jnp.bfloat16)
    tail_heads = jnp.einsum(
        "bij,bjc->bic", tail_pick, prior_heads, preferred_element_type=jnp.float32
    ).astype(jnp.bfloat16)
    pick_local = lax.dynamic_slice_in_dim(tail_pick, head_index * local_nodes, local_nodes, 2)
    tail_part = jnp.einsum(
        "bij,bjc->bic", pick_local, prior_groups, preferred_element_type=jnp.float32
    )
    tail_groups = lax.psum(tail_part.astype(jnp.bfloat16), "head")
    old_sums = jnp.einsum(
        "btj,bjh->bth", old_tree.astype(jnp.float32), old_steps * decay_rates, precision=highest
    )
    chosen_sum = jnp.sum(jnp.where(chosen_hot[:, :, None], old_sums, 0.0), axis=1)
    kept_weight = (
        jnp.where(
            lineage[:, :, None],
            jnp.exp(jnp.where(lineage[:, :, None], chosen_sum[:, None, :] - old_sums, 0.0)),
            0.0,
        )
        * old_steps
    )
    weighted = (
        (
            kept_weight[..., None]
            * old_heads.reshape(reqs_dev, NODES, local_heads, HEAD_DIM).astype(jnp.float32)
        )
        .astype(jnp.bfloat16)
        .reshape(reqs_dev, NODES, span_groups, span_heads, HEAD_DIM)
    )
    key_slice = lax.dynamic_slice_in_dim(
        old_keys, first_group * STATE, span_groups * STATE, 2
    ).reshape(reqs_dev, NODES, span_groups, STATE)
    update = jnp.einsum(
        "bjgqp,bjgn->bgqpn", weighted, key_slice, preferred_element_type=jnp.float32
    )
    carry_state = (
        jnp.exp(chosen_sum).reshape(reqs_dev, span_groups, span_heads, 1, 1)
        * old_state.reshape(reqs_dev, span_groups, span_heads, HEAD_DIM, STATE).astype(jnp.float32)
        + update
    ).astype(jnp.bfloat16)
    head_rows, gate_rows, step_rows = (
        lax.all_to_all(tree_heads, "head", split_axis=1, concat_axis=0, tiled=True),
        lax.all_to_all(tree_gates, "head", split_axis=1, concat_axis=0, tiled=True),
        lax.all_to_all(tree_steps, "head", split_axis=1, concat_axis=0, tiled=True),
    )
    group_rows = lax.all_gather(tree_groups, "head", axis=0, tiled=True)
    head_rows = head_rows.reshape(reqs_dev, NODES, -1)
    gate_rows = gate_rows.reshape(reqs_dev, NODES, span_groups, span_heads, HEAD_DIM)
    step_rows = step_rows.reshape(reqs_dev, NODES, local_heads)
    group_rows = group_rows.reshape(reqs_dev, NODES, -1)
    moved = (
        lax.all_to_all(
            place_slots(carry_state, send_pos, slot_count),
            "req",
            split_axis=0,
            concat_axis=0,
            tiled=True,
        ),
        lax.all_to_all(
            place_slots(tail_heads, send_pos, slot_count),
            "req",
            split_axis=0,
            concat_axis=0,
            tiled=True,
        ),
        lax.all_to_all(
            place_slots(tail_groups, send_pos, slot_count),
            "req",
            split_axis=0,
            concat_axis=0,
            tiled=True,
        ),
    )
    held_state = jnp.take(moved[0], recv_pos, axis=0)
    conv_heads = tree_conv(
        head_rows, jnp.take(moved[1], recv_pos, axis=0), new_tree, kernel_heads, shift_heads
    )
    conv_groups = tree_conv(
        group_rows, jnp.take(moved[2], recv_pos, axis=0), new_tree, kernel_groups, shift_groups
    )
    own_keys = lax.dynamic_slice_in_dim(conv_groups, first_group * STATE, span_groups * STATE, 2)
    own_queries = lax.dynamic_slice_in_dim(
        conv_groups, key_width + first_group * STATE, span_groups * STATE, 2
    )
    conv_heads, own_keys, own_queries = (conv_heads, own_keys, own_queries)
    query_four = own_queries.reshape(reqs_dev, NODES, span_groups, STATE)
    carried = jnp.einsum(
        "btgn,bgqpn->btgqp", query_four, held_state, preferred_element_type=jnp.float32
    )
    key_four = own_keys.reshape(reqs_dev, NODES, span_groups, STATE)
    step_sizes = jax.nn.softplus(step_rows.astype(jnp.float32) + step_bias)
    decay_sum = jnp.einsum(
        "btj,bjh->bth", new_tree.astype(jnp.float32), step_sizes * decay_rates, precision=highest
    )
    intersection = jnp.einsum(
        "btgn,bjgn->btjg", query_four, key_four, preferred_element_type=jnp.float32
    )
    lineage_new = (new_tree == 1)[:, :, :, None]
    decay_gap = decay_sum[:, :, None, :] - decay_sum[:, None, :, :]
    decays = jnp.where(lineage_new, jnp.exp(jnp.where(lineage_new, decay_gap, 0.0)), 0.0)
    mixing = (
        decays.reshape(reqs_dev, NODES, NODES, span_groups, span_heads)
        * intersection[..., None]
        * step_sizes.reshape(reqs_dev, 1, NODES, span_groups, span_heads)
    ).astype(jnp.bfloat16)
    values = conv_heads.reshape(reqs_dev, NODES, span_groups, span_heads, HEAD_DIM)
    inner_part = jnp.einsum(
        "btjgq,bjgqp->btgqp", mixing, values, preferred_element_type=jnp.float32
    )
    output = (
        inner_part
        + jnp.exp(decay_sum).reshape(reqs_dev, NODES, span_groups, span_heads, 1) * carried
        + skip_gain.reshape(1, 1, span_groups, span_heads, 1) * values.astype(jnp.float32)
    )
    gated_out = output * jax.nn.silu(gate_rows.astype(jnp.float32))
    group_power = jnp.sum(gated_out * gated_out, axis=(3, 4))
    zero_index = jnp.zeros((), jnp.int32)
    power_full = lax.dynamic_update_slice(
        jnp.zeros((reqs_dev, NODES, GROUPS), jnp.float32),
        group_power,
        (zero_index, zero_index, first_group),
    )
    power_total = lax.psum(power_full, "head")
    power_own = lax.dynamic_slice_in_dim(power_total, first_group, span_groups, 2)
    scale_factor = lax.rsqrt(power_own / (per_group * HEAD_DIM) + EPSILON)
    normed = (
        gated_out
        * scale_factor[..., None, None]
        * norm_gain.reshape(1, 1, span_groups, span_heads, HEAD_DIM)
    )
    return normed.reshape(reqs_dev * NODES, local_heads * HEAD_DIM).astype(jnp.bfloat16)


def solution(mesh):
    placed = (
        P(("req", "head"), None),
        P(("req", "head"), None),
        P(("req", "head"), None),
        P(("req", "head"), None),
        P("req", None, None),
        P(None, "head"),
        P("head"),
        P(),
        P(),
        P("head"),
        P("head"),
        P("head"),
        P("head"),
        P("req", "head", None, None),
        P("req", None, "head"),
        P("req", None, None),
        P("req", None, "head"),
        P("req", None, "head"),
        P("req", "head", None),
        P("req", None, None),
        P("req"),
        P(),
    )
    return jax.shard_map(
        shards, mesh=mesh, in_specs=placed, out_specs=P("req", "head"), check_vma=False
    )
```

profile of v0, /device:TPU:32, one launch (start us, length us, event | category | flops | bytes accessed | tf_op | source)
XLA Modules:
  0.0 639.1 jit_solution(553130558290788781)
XLA Ops:
  6.5 0.9 copy.90
  7.4 0.7 reshape.611
  8.2 7.0 %all-to-all-start.2 = ((bf16[16,2,128]{2,1,0:T(2,128)(2,1)}), bf16[16,2,128]{2,1,0:T(2,128)(2,1)S(1)}, u32[]{:S(2)}, u32[]{:S(2)}) async-start(bf16[16,2,128]{2,1,0:T(2,128)(2,1)} %reshape.611), calls=%async_computation.2 | async-start | bytes 16384 | tf_op jit(solution)/shard_map/all_to_all | solution.py:148
  15.2 0.7 iota_compare_fusion.9
  16.0 1.2 fusion.81
  17.2 0.8 broadcast_add_fusion.4
  18.2 2.0 convolution_convert_fusion
  20.3 0.8 reshape.530
  21.6 1.4 convolution_convert_fusion.1
  23.1 0.8 gather_fusion.1
  23.8 1.0 select_select_fusion.1
  24.8 1.2 exponential_negate_fusion
  26.0 1.6 reshape.543
  27.7 1.9 copy.134
  29.6 1.9 copy.133
  31.5 8.6 %all-to-all-start.1 = ((bf16[32,3,1024]{2,1,0:T(4,128)(2,1)}), bf16[32,3,1024]{2,1,0:T(4,128)(2,1)}, u32[]{:S(2)}, u32[]{:S(2)}) async-start(bf16[32,3,1024]{2,1,0:T(4,128)(2,1)} %select_select_fusion.1), calls=%async_computation.1 | async-start | bytes 524288 | tf_op jit(solution)/shard_map/all_to_all | solution.py:163
  40.3 0.8 broadcast_multiply_fusion
  41.1 1.0 select_reduce_fusion.1
  42.3 7.5 %all-to-all-done.1 = bf16[32,3,1024]{2,1,0:T(4,128)(2,1)} async-done(((bf16[32,3,1024]{2,1,0:T(4,128)(2,1)}), bf16[32,3,1024]{2,1,0:T(4,128)(2,1)}, u32[]{:S(2)}, u32[]{:S(2)}) %all-to-all-start.1) | async-done | bytes 196640 | tf_op jit(solution)/shard_map/all_to_all | solution.py:163
  49.7 7.3 %all-to-all-start = ((bf16[16,16,1024]{2,0,1:T(8,128)(2,1)}), bf16[16,16,1024]{2,0,1:T(8,128)(2,1)}, u32[]{:S(2)}, u32[]{:S(2)}) async-start(bf16[16,16,1024]{2,0,1:T(8,128)(2,1)} %bitcast.122), calls=%async_computation | async-start | bytes 1048576 | tf_op jit(solution)/shard_map/all_to_all | solution.py:146
  57.0 5.6 add_convert_fusion
  62.7 9.3 %gather_fusion.5 = bf16[32,16,64,256]{3,2,1,0:T(8,128)(2,1)} fusion(bf16[8,16,64,256]{3,2,1,0:T(8,128)(2,1)} %add_convert_fusion, s32[1024]{0:T(1024)S(1)} %pad_clamp_fusion.1), kind=kCustom, calls=%fused_computation.5 | custom fusion | bytes 33554560 | tf_op jit(solution)/shard_map/jit(_take)/gather | solution.py:40
  72.0 47.8 %all-reduce.2.cloned.1.call-done = bf16[8,3,4096]{2,1,0:T(4,128)(2,1)} async-done(((bf16[8,3,4096]{2,1,0:T(4,128)(2,1)}), bf16[8,3,4096]{2,1,0:T(4,128)(2,1)}) %all-reduce.2.cloned.1.call-update) | async-done | bytes 196624 | tf_op jit(solution)/shard_map/psum | solution.py:113
  119.7 2.4 gather_fusion.3
  122.1 5.0 all-to-all-start.5
  127.2 1.7 select_select_fusion
  128.9 8.4 %all-to-all-done.5 = bf16[16,16,1024]{2,0,1:T(8,128)(2,1)S(1)} async-done(((bf16[16,16,1024]{2,0,1:T(8,128)(2,1)}), bf16[16,16,1024]{2,0,1:T(8,128)(2,1)S(1)}, u32[]{:S(2)}, u32[]{:S(2)}) %all-to-all-start.5) | async-done | bytes 524320 | tf_op jit(solution)/shard_map/all_to_all | solution.py:147
  137.3 7.5 %all-to-all-start.3 = ((bf16[32,3,4096]{2,1,0:T(4,128)(2,1)}), bf16[32,3,4096]{2,1,0:T(4,128)(2,1)S(1)}, u32[]{:S(2)}, u32[]{:S(2)}) async-start(bf16[32,3,4096]{2,1,0:T(4,128)(2,1)} %select_select_fusion), calls=%async_computation.3 | async-start | bytes 2097152 | tf_op jit(solution)/shard_map/all_to_all | solution.py:170
  144.8 14.3 %fusion.1 = bf16[32,1,16,64,256]{4,3,2,1,0:T(8,128)(2,1)} fusion(bf16[32,16,64,256]{3,2,1,0:T(8,128)(2,1)} %gather_fusion.5, pred[32]{0:T(512)(128)(4,1)S(1)} %compare_and_fusion.10, pred[32]{0:T(512)(128)(4,1)S(1)} %copy-done.19), kind=kLoop, calls=%fused_computation.9 | loop fusion | flops 16777216 | bytes 33554496 | tf_op jit(solution)/shard_map/jit(_where)/select_n | solution.py:41
  159.1 10.3 %all-to-all-done.3 = bf16[32,3,4096]{2,1,0:T(4,128)(2,1)S(1)} async-done(((bf16[32,3,4096]{2,1,0:T(4,128)(2,1)}), bf16[32,3,4096]{2,1,0:T(4,128)(2,1)S(1)}, u32[]{:S(2)}, u32[]{:S(2)}) %all-to-all-start.3) | async-done | bytes 786464 | tf_op jit(solution)/shard_map/all_to_all | solution.py:170
  169.4 0.9 copy-done.5
  170.3 6.8 %all-to-all-start.4 = ((bf16[32,1,16,64,256]{4,3,2,1,0:T(8,128)(2,1)}), bf16[32,1,16,64,256]{4,3,2,1,0:T(8,128)(2,1)}, u32[]{:S(2)}, u32[]{:S(2)}) async-start(bf16[32,1,16,64,256]{4,3,2,1,0:T(8,128)(2,1)} %fusion.1), calls=%async_computation.4 | async-start | bytes 33554432 | tf_op jit(solution)/shard_map/all_to_all | solution.py:156
  177.4 0.5 all-gather.2.cloned.1.call-update
  178.3 0.6 gather_fusion
  179.4 0.6 slice_convert_fusion
  180.1 0.3 fusion.82
  180.4 1.6 gather_fusion.2
  182.0 1.4 fusion.45
  183.4 1.4 fusion.43
  184.8 1.4 fusion.41
  186.1 0.4 fusion.16
  186.5 0.4 fusion.17
  187.0 1.8 multiply_convert_fusion.4
  188.7 0.6 reshape.544
  189.3 1.7 reshape.532
  191.0 1.2 convert_bitcast_fusion
  192.1 1.9 reshape.545
  194.0 2.1 gather_fusion.4
  196.1 31.9 %all-gather.2.cloned.1.call-done = bf16[256,4096]{1,0:T(8,128)(2,1)} async-done(((bf16[16,4096]{1,0:T(8,128)(2,1)}), bf16[256,4096]{1,0:T(8,128)(2,1)}) %all-gather.2.cloned.1.call-update) | async-done | bytes 2097168 | tf_op jit(solution)/shard_map/all_gather | solution.py:150
  228.0 2.5 fusion.42
  230.5 0.7 fusion.40
  231.3 0.8 fusion.44
  232.1 0.9 fusion.5
  233.0 1.5 fusion.4
  234.6 1.7 multiply_convert_fusion
  236.3 1.4 copy-done.11
  238.0 301.8 %all-to-all-done.4 = bf16[32,1,16,64,256]{4,3,2,1,0:T(8,128)(2,1)} async-done(((bf16[32,1,16,64,256]{4,3,2,1,0:T(8,128)(2,1)}), bf16[32,1,16,64,256]{4,3,2,1,0:T(8,128)(2,1)}, u32[]{:S(2)}, u32[]{:S(2)}) %all-to-all-start.4) | async-done | bytes 16777248 | tf_op jit(solution)/shard_map/all_to_all | solution.py:156
  539.8 8.6 %gather_fusion.6 = bf16[8,16,64,256]{3,2,1,0:T(8,128)(2,1)} fusion(bf16[32,16,64,256]{3,2,1,0:T(8,128)(2,1)} %bitcast.31, s32[1024]{0:T(1024)} %copy-done.17), kind=kCustom, calls=%fused_computation.6 | custom fusion | bytes 8388640 | tf_op jit(solution)/shard_map/jit(_take)/gather | solution.py:178
  548.4 4.7 fusion.8
  553.2 4.7 multiply_reduce_fusion
  557.8 70.6 %psum.15 = f32[8,32,8]{1,0,2:T(8,128)S(1)} all-reduce(f32[8,32,8]{1,0,2:T(8,128)S(1)} %bitcast_dynamic-update-slice_fusion), channel_id=1, replica_groups=mesh['req'=16,'head'=16] {'head'}, use_global_device_ids=true, to_apply=%region_11.12 | all-reduce | flops 2048 | bytes 16384 | tf_op jit(solution)/shard_map/psum | solution.py:227
  628.4 1.9 multiply_convert_fusion.1
  630.3 0.4 copy.104
  630.8 1.5 convert_element_type.240
  (94 shorter events, 2.5 us)
Async XLA Ops:
  6.5 50.5 %copy-start = (bf16[8,32,2048]{2,1,0:T(8,128)(2,1)S(1)}, bf16[8,32,2048]{2,1,0:T(8,128)(2,1)}, u32[]{:S(2)}) copy-start(bf16[8,32,2048]{2,1,0:T(8,128)(2,1)} %param.37) | copy-start | bytes 3145732
  8.2 23.3 %all-to-all-start.2 = ((bf16[16,2,128]{2,1,0:T(2,128)(2,1)}), bf16[16,2,128]{2,1,0:T(2,128)(2,1)S(1)}, u32[]{:S(2)}, u32[]{:S(2)}) async-start(bf16[16,2,128]{2,1,0:T(2,128)(2,1)} %reshape.611), calls=%async_computation.2 | async-start | bytes 16384 | tf_op jit(solution)/shard_map/all_to_all | solution.py:148
  15.2 104.5 %all-reduce.2.cloned.1.call-start = ((), (), s32[]{:S(2)}) async-start(), calls=%async_computation.7 | async-start | bytes 524288 | tf_op jit(solution)/shard_map/psum | solution.py:113
  16.0 2.0 copy-start.20
  18.2 22.1 %copy-start.9 = (f32[8,32,16]{1,2,0:T(8,128)S(1)}, f32[8,32,16]{1,2,0:T(8,128)}, u32[]{:S(2)}) copy-start(f32[8,32,16]{1,2,0:T(8,128)} %param.38) | copy-start | bytes 49156
  20.2 20.9 %copy-start.8 = (s32[8,32,32]{2,1,0:T(8,128)S(1)}, s32[8,32,32]{2,1,0:T(8,128)}, u32[]{:S(2)}) copy-start(s32[8,32,32]{2,1,0:T(8,128)} %param.41) | copy-start | bytes 98308
  21.6 18.5 %copy-start.18 = (pred[32]{0:T(512)(128)(4,1)}, pred[32]{0:T(512)(128)(4,1)S(1)}, u32[]{:S(2)}) copy-start(pred[32]{0:T(512)(128)(4,1)S(1)} %fusion.68) | copy-start | bytes 100
  31.5 18.3 %all-to-all-start.1 = ((bf16[32,3,1024]{2,1,0:T(4,128)(2,1)}), bf16[32,3,1024]{2,1,0:T(4,128)(2,1)}, u32[]{:S(2)}, u32[]{:S(2)}) async-start(bf16[32,3,1024]{2,1,0:T(4,128)(2,1)} %select_select_fusion.1), calls=%async_computation.1 | async-start | bytes 524288 | tf_op jit(solution)/shard_map/all_to_all | solution.py:163
  49.7 72.4 %all-to-all-start = ((bf16[16,16,1024]{2,0,1:T(8,128)(2,1)}), bf16[16,16,1024]{2,0,1:T(8,128)(2,1)}, u32[]{:S(2)}, u32[]{:S(2)}) async-start(bf16[16,16,1024]{2,0,1:T(8,128)(2,1)} %bitcast.122), calls=%async_computation | async-start | bytes 1048576 | tf_op jit(solution)/shard_map/all_to_all | solution.py:146
  62.7 64.5 %copy-start.19 = (pred[32]{0:T(512)(128)(4,1)S(1)}, pred[32]{0:T(512)(128)(4,1)}, u32[]{:S(2)}) copy-start(pred[32]{0:T(512)(128)(4,1)} %copy-done.18) | copy-start | bytes 100
  122.1 15.1 %all-to-all-start.5 = ((bf16[16,16,1024]{2,0,1:T(8,128)(2,1)}), bf16[16,16,1024]{2,0,1:T(8,128)(2,1)S(1)}, u32[]{:S(2)}, u32[]{:S(2)}) async-start(bf16[16,16,1024]{2,0,1:T(8,128)(2,1)} %bitcast.116), calls=%async_computation.5 | async-start | bytes 1048576 | tf_op jit(solution)/shard_map/all_to_all | solution.py:147
  137.3 21.8 %copy-start.3 = (bf16[16,16,1024]{2,0,1:T(8,128)(2,1)}, bf16[16,16,1024]{2,0,1:T(8,128)(2,1)S(1)}, u32[]{:S(2)}) copy-start(bf16[16,16,1024]{2,0,1:T(8,128)(2,1)S(1)} %all-to-all-done.5) | copy-start | bytes 1572868
  137.3 32.1 %all-to-all-start.3 = ((bf16[32,3,4096]{2,1,0:T(4,128)(2,1)}), bf16[32,3,4096]{2,1,0:T(4,128)(2,1)S(1)}, u32[]{:S(2)}, u32[]{:S(2)}) async-start(bf16[32,3,4096]{2,1,0:T(4,128)(2,1)} %select_select_fusion), calls=%async_computation.3 | async-start | bytes 2097152 | tf_op jit(solution)/shard_map/all_to_all | solution.py:170
  159.0 19.1 %copy-start.22 = (s32[128]{0:T(128)S(1)}, s32[128]{0:T(128)}, u32[]{:S(2)}) copy-start(s32[128]{0:T(128)} %param.43) | copy-start | bytes 1540
  159.0 20.0 %copy-start.6 = (s32[8,32,32]{2,1,0:T(8,128)S(1)}, s32[8,32,32]{2,1,0:T(8,128)}, u32[]{:S(2)}) copy-start(s32[8,32,32]{2,1,0:T(8,128)} %param.26) | copy-start | bytes 98308
  159.0 20.2 %copy-start.21 = (f32[1024]{0:T(1024)S(1)}, f32[1024]{0:T(1024)}, u32[]{:S(2)}) copy-start(f32[1024]{0:T(1024)} %param.34) | copy-start | bytes 12292
  159.0 20.3 %copy-start.12 = (bf16[4,1024]{1,0:T(4,128)(2,1)S(1)}, bf16[4,1024]{1,0:T(4,128)(2,1)}, u32[]{:S(2)}) copy-start(bf16[4,1024]{1,0:T(4,128)(2,1)} %param.27) | copy-start | bytes 24580
  159.1 20.3 %copy-start.10 = (bf16[4,4096]{1,0:T(4,128)(2,1)S(1)}, bf16[4,4096]{1,0:T(4,128)(2,1)}, u32[]{:S(2)}) copy-start(bf16[4,4096]{1,0:T(4,128)(2,1)} %param.29) | copy-start | bytes 98308
  169.4 0.9 copy-start.5
  170.3 369.5 %all-to-all-start.4 = ((bf16[32,1,16,64,256]{4,3,2,1,0:T(8,128)(2,1)}), bf16[32,1,16,64,256]{4,3,2,1,0:T(8,128)(2,1)}, u32[]{:S(2)}, u32[]{:S(2)}) async-start(bf16[32,1,16,64,256]{4,3,2,1,0:T(8,128)(2,1)} %fusion.1), calls=%async_computation.4 | async-start | bytes 33554432 | tf_op jit(solution)/shard_map/all_to_all | solution.py:156
  177.2 50.9 %all-gather.2.cloned.1.call-start = ((), (), s32[]{:S(2)}) async-start(), calls=%async_computation.6 | async-start | bytes 2228224 | tf_op jit(solution)/shard_map/all_gather | solution.py:150
  179.0 8.0 %copy-start.15 = (pred[8]{0:T(512)(128)(4,1)}, pred[8]{0:T(512)(128)(4,1)S(1)}, u32[]{:S(2)}) copy-start(pred[8]{0:T(512)(128)(4,1)S(1)} %compare_and_fusion.11) | copy-start | bytes 28
  179.3 7.6 %copy-start.17 = (s32[1024]{0:T(1024)}, s32[1024]{0:T(1024)S(1)}, u32[]{:S(2)}) copy-start(s32[1024]{0:T(1024)S(1)} %pad_clamp_fusion) | copy-start | bytes 12292
  183.3 3.6 copy-start.23
  228.0 2.5 copy-start.2
  231.3 0.8 copy-start.16
  232.1 0.9 copy-start.14
  233.0 1.6 copy-start.13
  236.3 1.4 copy-start.11
  548.4 4.7 copy-start.4
  548.4 4.7 copy-start.7
  548.4 4.7 copy-start.24
  553.2 79.1 %copy-start.1 = (bf16[8,32,2048]{2,1,0:T(8,128)(2,1)S(1)}, bf16[8,32,2048]{2,1,0:T(8,128)(2,1)}, u32[]{:S(2)}) copy-start(bf16[8,32,2048]{2,1,0:T(8,128)(2,1)} %param.37) | copy-start | bytes 3145732
Sparse Core Ops, SparseCore 0:
  20.4 99.3 all-reduce.1
  180.4 47.5 all-gather.1
where the time goes:
time: 641 us; the launch traced here: 639 us
  waiting for transfers between devices  408 us (64%)
  blocking collectives  70.6 us (11%)
  local copies, waits for them, and re-layouts  42.5 us (7%)
  starting transfers between devices  42.5 us (7%)
  matrix products  34.7 us (5%)
  other arithmetic  26.6 us (4%)
  between operations  14.1 us (2%)
    all_to_all x1, waiting for transfers between devices, shards(): lax.all_to_all(place_slots(carry_state, send_pos, slot_count), 'req', spl...  302 us
    psum x1, blocking collectives, shards(): power_total = lax.psum(power_full, 'head')  70.6 us
    psum x1, waiting for transfers between devices, shards(): tail_groups = lax.psum(tail_part.astype(jnp.bfloat16), 'head')  47.8 us
    all_gather x1, waiting for transfers between devices, shards(): group_rows = lax.all_gather(tree_groups, 'head', axis=0, tiled=True)  31.9 us
    select_n x3, other arithmetic, place_slots(): return jnp.where(filled, taken, jnp.zeros_like(taken))  16.9 us
  transfers between devices with their start and end apart: 8, of which 6 were waited for; matrix products, arithmetic and copies ran while one was open for 12% of the time, Pallas kernels for 0%

commit v1 on v0

--- a/solution.py
+++ b/solution.py
@@ -147,7 +147,9 @@
         lax.all_to_all(tree_gates, "head", split_axis=1, concat_axis=0, tiled=True),
         lax.all_to_all(tree_steps, "head", split_axis=1, concat_axis=0, tiled=True),
     )
-    group_rows = lax.all_gather(tree_groups, "head", axis=0, tiled=True)
+    group_rows = jnp.concatenate(
+        lax.all_to_all(jnp.stack([tree_groups] * lax.axis_size("head")), "head", 0, 0), axis=0
+    )
     head_rows = head_rows.reshape(reqs_dev, NODES, -1)
     gate_rows = gate_rows.reshape(reqs_dev, NODES, span_groups, span_heads, HEAD_DIM)
     step_rows = step_rows.reshape(reqs_dev, NODES, local_heads)

time: 641 us -> 704 us (1.098)
  waiting for transfers between devices: 408 us -> 469 us
    psum x1, waiting for transfers between devices: 47.8 us -> 96 us  [shards(): tail_groups = lax.psum(tail_part.astype(jnp.bfloat16), 'head')]
    all_to_all x1, waiting for transfers between devices: 302 us -> 337 us  [shards(): lax.all_to_all(place_slots(carry_state, send_pos, slot_count), 'req', spl...]
    all_gather x1 -> x0, waiting for transfers between devices: 31.9 us -> none  [shards(): group_rows = lax.all_gather(tree_groups, 'head', axis=0, tiled=True)]
    all_to_all x1, waiting for transfers between devices: 10.3 us -> 19.1 us  [shards(): lax.all_to_all(place_slots(tail_groups, send_pos, slot_count), 'req', spl...]
  transfers between devices with their start and end apart: 8 -> 8, of which waited for: 6 -> 6; matrix products, arithmetic and copies ran while one was open for 12% -> 11% of each run, Pallas kernels for 0% -> 0%
where the time goes in v1:
time: 704 us; the launch traced here: 703 us
  waiting for transfers between devices  469 us (67%)
  blocking collectives  74.6 us (11%)
  local copies, waits for them, and re-layouts  46.7 us (7%)
  starting transfers between devices  46.1 us (7%)
  matrix products  28.1 us (4%)
  other arithmetic  24.3 us (3%)
  between operations  14.1 us (2%)
    all_to_all x1, waiting for transfers between devices, shards(): lax.all_to_all(place_slots(carry_state, send_pos, slot_count), 'req', spl...  337 us
    psum x1, waiting for transfers between devices, shards(): tail_groups = lax.psum(tail_part.astype(jnp.bfloat16), 'head')  96 us
    psum x1, blocking collectives, shards(): power_total = lax.psum(power_full, 'head')  74.6 us
    all_to_all x1, waiting for transfers between devices, shards(): lax.all_to_all(place_slots(tail_groups, send_pos, slot_count), 'req', spl...  19.1 us
    select_n x3, other arithmetic, place_slots(): return jnp.where(filled, taken, jnp.zeros_like(taken))  16.9 us
  transfers between devices with their start and end apart: 8, of which 6 were waited for; matrix products, arithmetic and copies ran while one was open for 11% of the time, Pallas kernels for 0%

profile of v1, /device:TPU:32, one launch (start us, length us, event | category | flops | bytes accessed | tf_op | source)
XLA Modules:
  0.0 702.7 jit_solution(17079442492796601729)
XLA Ops:
  6.5 0.9 copy.90
  7.5 0.7 reshape.609
  8.2 7.0 %all-to-all-start.2 = ((bf16[16,2,128]{2,1,0:T(2,128)(2,1)}), bf16[16,2,128]{2,1,0:T(2,128)(2,1)S(1)}, u32[]{:S(2)}, u32[]{:S(2)}) async-start(bf16[16,2,128]{2,1,0:T(2,128)(2,1)} %reshape.609), calls=%async_computation.2 | async-start | bytes 16384 | tf_op jit(solution)/shard_map/all_to_all | solution.py:148
  15.3 0.7 reshape.529
  16.6 0.7 iota_compare_fusion.9
  17.3 1.2 fusion.81
  18.5 0.8 broadcast_add_fusion.4
  19.4 1.4 convolution_convert_fusion.1
  20.9 0.8 gather_fusion.1
  21.6 1.0 select_select_fusion.1
  22.6 0.2 all-to-all-done.2
  22.8 8.6 %all-to-all-start.1 = ((bf16[32,3,1024]{2,1,0:T(4,128)(2,1)}), bf16[32,3,1024]{2,1,0:T(4,128)(2,1)S(1)}, u32[]{:S(2)}, u32[]{:S(2)}) async-start(bf16[32,3,1024]{2,1,0:T(4,128)(2,1)} %select_select_fusion.1), calls=%async_computation.1 | async-start | bytes 524288 | tf_op jit(solution)/shard_map/all_to_all | solution.py:165
  31.4 1.9 copy.134
  33.3 7.7 %all-to-all-done.1 = bf16[32,3,1024]{2,1,0:T(4,128)(2,1)S(1)} async-done(((bf16[32,3,1024]{2,1,0:T(4,128)(2,1)}), bf16[32,3,1024]{2,1,0:T(4,128)(2,1)S(1)}, u32[]{:S(2)}, u32[]{:S(2)}) %all-to-all-start.1) | async-done | bytes 196640 | tf_op jit(solution)/shard_map/all_to_all | solution.py:165
  41.0 0.7 copy-done.12
  41.7 7.0 all-to-all-start
  48.9 1.1 convolution_convert_fusion
  50.0 0.8 copy.133
  50.9 96.0 %all-reduce.2.cloned.1.call-done = bf16[8,3,4096]{2,1,0:T(4,128)(2,1)} async-done(((bf16[8,3,4096]{2,1,0:T(4,128)(2,1)}), bf16[8,3,4096]{2,1,0:T(4,128)(2,1)}) %all-reduce.2.cloned.1.call-update) | async-done | bytes 196624 | tf_op jit(solution)/shard_map/psum | solution.py:113
  146.9 2.4 gather_fusion.3
  149.3 5.2 all-to-all-start.6
  154.5 1.7 select_select_fusion
  156.3 8.3 %all-to-all-done.6 = bf16[16,16,1024]{2,0,1:T(8,128)(2,1)S(1)} async-done(((bf16[16,16,1024]{2,0,1:T(8,128)(2,1)}), bf16[16,16,1024]{2,0,1:T(8,128)(2,1)S(1)}, u32[]{:S(2)}, u32[]{:S(2)}) %all-to-all-start.6) | async-done | bytes 524320 | tf_op jit(solution)/shard_map/all_to_all | solution.py:147
  164.6 7.5 %all-to-all-start.4 = ((bf16[32,3,4096]{2,1,0:T(4,128)(2,1)}), bf16[32,3,4096]{2,1,0:T(4,128)(2,1)S(1)}, u32[]{:S(2)}, u32[]{:S(2)}) async-start(bf16[32,3,4096]{2,1,0:T(4,128)(2,1)} %select_select_fusion), calls=%async_computation.4 | async-start | bytes 2097152 | tf_op jit(solution)/shard_map/all_to_all | solution.py:172
  172.1 2.8 reshape.541
  174.9 0.5 exponential_negate_fusion
  175.7 0.8 broadcast_multiply_fusion
  176.5 1.1 select_reduce_fusion.1
  177.7 19.1 %all-to-all-done.4 = bf16[32,3,4096]{2,1,0:T(4,128)(2,1)S(1)} async-done(((bf16[32,3,4096]{2,1,0:T(4,128)(2,1)}), bf16[32,3,4096]{2,1,0:T(4,128)(2,1)S(1)}, u32[]{:S(2)}, u32[]{:S(2)}) %all-to-all-start.4) | async-done | bytes 786464 | tf_op jit(solution)/shard_map/all_to_all | solution.py:172
  196.7 2.6 stack.2
  199.3 3.7 all-to-all-start.3
  203.1 7.1 %add_convert_fusion = bf16[8,16,64,256]{3,2,1,0:T(8,128)(2,1)} fusion(bf16[8,16,64,256]{3,2,1,0:T(8,128)(2,1)} %param.35, f32[8,16]{1,0:T(8,128)S(1)} %exp.56, f32[8,32,16,64]{3,2,1,0:T(8,128)} %reshape.541, f32[8,32,16]{1,2,0:T(8,128)S(1)} %bitcast_multiply_fusion.1, bf16[8,32,2048]{2,1,0:T(8,128)(2,1)S(1)} %copy-done, s32[]{:T(128)S(6)} %select_n.269), kind=kOutput, calls=%fused_computation.10 | convolution fusion | flops 143130624 | bytes 9637892 | tf_op jit(solution)/shard_map/bjgqp,bjgn->bgqpn/dot_general | solution.py:137
  210.2 9.3 %gather_fusion.5 = bf16[32,16,64,256]{3,2,1,0:T(8,128)(2,1)} fusion(bf16[8,16,64,256]{3,2,1,0:T(8,128)(2,1)} %add_convert_fusion, s32[1024]{0:T(1024)S(1)} %pad_clamp_fusion.1), kind=kCustom, calls=%fused_computation.5 | custom fusion | bytes 33554560 | tf_op jit(solution)/shard_map/jit(_take)/gather | solution.py:40
  219.5 14.3 %fusion.1 = bf16[32,1,16,64,256]{4,3,2,1,0:T(8,128)(2,1)} fusion(bf16[32,16,64,256]{3,2,1,0:T(8,128)(2,1)} %gather_fusion.5, pred[32]{0:T(512)(128)(4,1)S(1)} %compare_and_fusion.10, pred[32]{0:T(512)(128)(4,1)S(1)} %copy-done.22), kind=kLoop, calls=%fused_computation.9 | loop fusion | flops 16777216 | bytes 33554496 | tf_op jit(solution)/shard_map/jit(_where)/select_n | solution.py:41
  233.8 7.1 %all-to-all-start.5 = ((bf16[32,1,16,64,256]{4,3,2,1,0:T(8,128)(2,1)}), bf16[32,1,16,64,256]{4,3,2,1,0:T(8,128)(2,1)}, u32[]{:S(2)}, u32[]{:S(2)}) async-start(bf16[32,1,16,64,256]{4,3,2,1,0:T(8,128)(2,1)} %fusion.1), calls=%async_computation.5 | async-start | bytes 33554432 | tf_op jit(solution)/shard_map/all_to_all | solution.py:158
  241.5 0.6 gather_fusion
  242.3 0.6 slice_convert_fusion
  243.0 0.3 fusion.82
  243.3 1.6 gather_fusion.2
  244.9 0.3 fusion.45
  245.3 0.3 fusion.43
  245.6 0.3 fusion.41
  246.0 0.4 fusion.16
  246.4 0.4 fusion.17
  246.8 1.5 multiply_convert_fusion.4
  248.4 2.7 reshape.542
  251.1 2.5 reshape.531
  253.6 1.2 convert_bitcast_fusion
  254.7 1.9 reshape.543
  256.7 2.1 gather_fusion.4
  258.8 0.8 fusion.42
  259.6 0.7 fusion.40
  260.3 0.7 fusion.44
  261.1 0.9 fusion.5
  262.0 1.5 fusion.4
  263.6 1.7 multiply_convert_fusion
  265.6 337.5 %all-to-all-done.5 = bf16[32,1,16,64,256]{4,3,2,1,0:T(8,128)(2,1)} async-done(((bf16[32,1,16,64,256]{4,3,2,1,0:T(8,128)(2,1)}), bf16[32,1,16,64,256]{4,3,2,1,0:T(8,128)(2,1)}, u32[]{:S(2)}, u32[]{:S(2)}) %all-to-all-start.5) | async-done | bytes 16777248 | tf_op jit(solution)/shard_map/all_to_all | solution.py:158
  603.0 8.7 %gather_fusion.6 = bf16[8,16,64,256]{3,2,1,0:T(8,128)(2,1)} fusion(bf16[32,16,64,256]{3,2,1,0:T(8,128)(2,1)} %bitcast.31, s32[1024]{0:T(1024)} %copy-done.20), kind=kCustom, calls=%fused_computation.6 | custom fusion | bytes 8388640 | tf_op jit(solution)/shard_map/jit(_take)/gather | solution.py:180
  611.7 4.5 fusion.8
  616.3 2.7 multiply_reduce_fusion
  619.0 74.6 %psum.15 = f32[8,32,8]{1,0,2:T(8,128)S(1)} all-reduce(f32[8,32,8]{1,0,2:T(8,128)S(1)} %bitcast_dynamic-update-slice_fusion), channel_id=1, replica_groups=mesh['req'=16,'head'=16] {'head'}, use_global_device_ids=true, to_apply=%region_11.12 | all-reduce | flops 2048 | bytes 16384 | tf_op jit(solution)/shard_map/psum | solution.py:229
  693.6 0.3 multiply_convert_fusion.1
  693.9 0.4 copy.104
  694.4 1.5 convert_element_type.240
  (104 shorter events, 2.3 us)
Async XLA Ops:
  6.5 196.5 %copy-start = (bf16[8,32,2048]{2,1,0:T(8,128)(2,1)S(1)}, bf16[8,32,2048]{2,1,0:T(8,128)(2,1)}, u32[]{:S(2)}) copy-start(bf16[8,32,2048]{2,1,0:T(8,128)(2,1)} %param.37) | copy-start | bytes 3145732
  6.5 42.4 %copy-start.26 = (bf16[8,2,4096]{2,1,0:T(2,128)(2,1)S(1)}, bf16[8,2,4096]{2,1,0:T(2,128)(2,1)}, u32[]{:S(2)}) copy-start(bf16[8,2,4096]{2,1,0:T(2,128)(2,1)} %param.40) | copy-start | bytes 393220
  6.5 43.5 %copy-start.10 = (bf16[16,16384]{1,0:T(8,128)(2,1)S(1)}, bf16[16,16384]{1,0:T(8,128)(2,1)}, u32[]{:S(2)}) copy-start(bf16[16,16384]{1,0:T(8,128)(2,1)} %param.23) | copy-start | bytes 1572868
  8.2 14.6 %all-to-all-start.2 = ((bf16[16,2,128]{2,1,0:T(2,128)(2,1)}), bf16[16,2,128]{2,1,0:T(2,128)(2,1)S(1)}, u32[]{:S(2)}, u32[]{:S(2)}) async-start(bf16[16,2,128]{2,1,0:T(2,128)(2,1)} %reshape.609), calls=%async_computation.2 | async-start | bytes 16384 | tf_op jit(solution)/shard_map/all_to_all | solution.py:148
  16.6 137.9 %copy-start.21 = (pred[32]{0:T(512)(128)(4,1)}, pred[32]{0:T(512)(128)(4,1)S(1)}, u32[]{:S(2)}) copy-start(pred[32]{0:T(512)(128)(4,1)S(1)} %fusion.68) | copy-start | bytes 100
  17.3 1.2 copy-start.23
  22.8 18.2 %all-to-all-start.1 = ((bf16[32,3,1024]{2,1,0:T(4,128)(2,1)}), bf16[32,3,1024]{2,1,0:T(4,128)(2,1)S(1)}, u32[]{:S(2)}, u32[]{:S(2)}) async-start(bf16[32,3,1024]{2,1,0:T(4,128)(2,1)} %select_select_fusion.1), calls=%async_computation.1 | async-start | bytes 524288 | tf_op jit(solution)/shard_map/all_to_all | solution.py:165
  41.0 0.7 copy-start.12
  41.7 107.6 %all-to-all-start = ((bf16[16,16,1024]{2,0,1:T(8,128)(2,1)}), bf16[16,16,1024]{2,0,1:T(8,128)(2,1)S(1)}, u32[]{:S(2)}, u32[]{:S(2)}) async-start(bf16[16,16,1024]{2,0,1:T(8,128)(2,1)} %bitcast.117), calls=%async_computation | async-start | bytes 1048576 | tf_op jit(solution)/shard_map/all_to_all | solution.py:146
  48.7 98.2 %all-reduce.2.cloned.1.call-start = ((), (), s32[]{:S(2)}) async-start(), calls=%async_computation.7 | async-start | bytes 524288 | tf_op jit(solution)/shard_map/psum | solution.py:113
  149.3 25.6 %copy-start.28 = (f32[16]{0:T(128)S(1)}, f32[16]{0:T(128)}, u32[]{:S(2)}) copy-start(f32[16]{0:T(128)} %param.31) | copy-start | bytes 196
  149.3 26.3 %copy-start.2 = (bf16[16,16,1024]{2,0,1:T(8,128)(2,1)}, bf16[16,16,1024]{2,0,1:T(8,128)(2,1)S(1)}, u32[]{:S(2)}) copy-start(bf16[16,16,1024]{2,0,1:T(8,128)(2,1)S(1)} %all-to-all-done) | copy-start | bytes 1572868
  149.3 26.3 %copy-start.13 = (f32[8,32,16]{1,2,0:T(8,128)S(1)}, f32[8,32,16]{1,2,0:T(8,128)}, u32[]{:S(2)}) copy-start(f32[8,32,16]{1,2,0:T(8,128)} %param.38) | copy-start | bytes 49156
  149.3 15.3 %all-to-all-start.6 = ((bf16[16,16,1024]{2,0,1:T(8,128)(2,1)}), bf16[16,16,1024]{2,0,1:T(8,128)(2,1)S(1)}, u32[]{:S(2)}, u32[]{:S(2)}) async-start(bf16[16,16,1024]{2,0,1:T(8,128)(2,1)} %bitcast.126), calls=%async_computation.6 | async-start | bytes 1048576 | tf_op jit(solution)/shard_map/all_to_all | solution.py:147
  154.5 21.9 %copy-start.11 = (s32[8,32,32]{2,1,0:T(8,128)S(1)}, s32[8,32,32]{2,1,0:T(8,128)}, u32[]{:S(2)}) copy-start(s32[8,32,32]{2,1,0:T(8,128)} %param.41) | copy-start | bytes 98308
  164.6 34.7 %copy-start.5 = (bf16[16,16,1024]{2,0,1:T(8,128)(2,1)}, bf16[16,16,1024]{2,0,1:T(8,128)(2,1)S(1)}, u32[]{:S(2)}) copy-start(bf16[16,16,1024]{2,0,1:T(8,128)(2,1)S(1)} %all-to-all-done.6) | copy-start | bytes 1572868
  164.6 32.1 %all-to-all-start.4 = ((bf16[32,3,4096]{2,1,0:T(4,128)(2,1)}), bf16[32,3,4096]{2,1,0:T(4,128)(2,1)S(1)}, u32[]{:S(2)}, u32[]{:S(2)}) async-start(bf16[32,3,4096]{2,1,0:T(4,128)(2,1)} %select_select_fusion), calls=%async_computation.4 | async-start | bytes 2097152 | tf_op jit(solution)/shard_map/all_to_all | solution.py:172
  196.7 2.6 copy-start.7
  199.3 34.5 %all-to-all-start.3 = ((bf16[16,16,4096]{2,1,0:T(8,128)(2,1)}), bf16[16,16,4096]{2,1,0:T(8,128)(2,1)S(1)}, u32[]{:S(2)}, u32[]{:S(2)}) async-start(bf16[16,16,4096]{2,1,0:T(8,128)(2,1)} %stack.2), calls=%async_computation.3 | async-start | bytes 4194304 | tf_op jit(solution)/shard_map/all_to_all | solution.py:151
  210.2 9.3 %copy-start.22 = (pred[32]{0:T(512)(128)(4,1)S(1)}, pred[32]{0:T(512)(128)(4,1)}, u32[]{:S(2)}) copy-start(pred[32]{0:T(512)(128)(4,1)} %copy-done.21) | copy-start | bytes 100
  233.8 7.3 %copy-start.8 = (s32[8,32,32]{2,1,0:T(8,128)S(1)}, s32[8,32,32]{2,1,0:T(8,128)}, u32[]{:S(2)}) copy-start(s32[8,32,32]{2,1,0:T(8,128)} %param.26) | copy-start | bytes 98308
  233.8 7.5 %copy-start.24 = (f32[1024]{0:T(1024)S(1)}, f32[1024]{0:T(1024)}, u32[]{:S(2)}) copy-start(f32[1024]{0:T(1024)} %param.34) | copy-start | bytes 12292
  233.8 7.6 %copy-start.25 = (s32[128]{0:T(128)S(1)}, s32[128]{0:T(128)}, u32[]{:S(2)}) copy-start(s32[128]{0:T(128)} %param.43) | copy-start | bytes 1540
  233.8 8.5 %copy-start.15 = (bf16[4,1024]{1,0:T(4,128)(2,1)S(1)}, bf16[4,1024]{1,0:T(4,128)(2,1)}, u32[]{:S(2)}) copy-start(bf16[4,1024]{1,0:T(4,128)(2,1)} %param.27) | copy-start | bytes 24580
  233.8 8.6 %copy-start.14 = (bf16[4,4096]{1,0:T(4,128)(2,1)S(1)}, bf16[4,4096]{1,0:T(4,128)(2,1)}, u32[]{:S(2)}) copy-start(bf16[4,4096]{1,0:T(4,128)(2,1)} %param.29) | copy-start | bytes 98308
  233.8 11.1 %copy-start.3 = (bf16[16,16,1024]{2,0,1:T(8,128)(2,1)S(1)}, bf16[16,16,1024]{2,0,1:T(8,128)(2,1)}, u32[]{:S(2)}) copy-start(bf16[16,16,1024]{2,0,1:T(8,128)(2,1)} %copy-done.2) | copy-start | bytes 1572868
  233.8 369.2 %all-to-all-start.5 = ((bf16[32,1,16,64,256]{4,3,2,1,0:T(8,128)(2,1)}), bf16[32,1,16,64,256]{4,3,2,1,0:T(8,128)(2,1)}, u32[]{:S(2)}, u32[]{:S(2)}) async-start(bf16[32,1,16,64,256]{4,3,2,1,0:T(8,128)(2,1)} %fusion.1), calls=%async_computation.5 | async-start | bytes 33554432 | tf_op jit(solution)/shard_map/all_to_all | solution.py:158
  242.2 4.6 copy-start.20
  242.3 4.5 copy-start.18
  245.3 1.5 copy-start.27
  260.3 0.8 copy-start.19
  261.1 0.9 copy-start.17
  262.0 1.6 copy-start.16
  611.7 4.5 copy-start.4
  611.7 4.5 copy-start.6
  611.7 4.5 copy-start.9
  611.7 4.5 copy-start.29
  616.2 79.6 %copy-start.1 = (bf16[8,32,2048]{2,1,0:T(8,128)(2,1)S(1)}, bf16[8,32,2048]{2,1,0:T(8,128)(2,1)}, u32[]{:S(2)}) copy-start(bf16[8,32,2048]{2,1,0:T(8,128)(2,1)} %param.37) | copy-start | bytes 3145732
Sparse Core Ops, SparseCore 0:
  52.7 94.1 all-reduce.1
